TPU v7x, 32 devices: a whole 2x2x4 slice. The times are simulated.
32 devices in a mesh: grp: 8 (over y, x, core), mem: 4 (over z).
Axes of the slice: x: 2, y: 2, z: 4, core: 2. Of those that a mesh axis runs over, the one named last changes fastest.
Arguments:
- points: float32 [16, 32768], P(None, ('grp', 'mem')), may hold values from -6 to 6
- residual: float32 [16, 32768], P(None, ('grp', 'mem')), may hold values from -6 to 6
- coef: float32 [16, 32768], P(None, ('grp', 'mem')), may hold values from -3 to 3
- block_of: int32 [32768], P(('grp', 'mem')), may hold values from 0 to 7, as said below
- order: int32 [2], replicated, may hold values from 0 to 7
- inverse: float32 [8, 4096, 4096], P('grp', 'mem'), may hold values from -1 to 2
Outputs:
- residual_out: float32 [16, 32768], P(None, ('grp', 'mem'))
- coef_out: float32 [16, 32768], P(None, ('grp', 'mem'))
Inputs may be any that keep to these rules, and one draw needn't show every extreme that they name: `block_of`: each run of 1024 consecutive points (the points of one device) holds exactly 128 points of every block.
All inputs are finite; a program needn't handle non-finite values.
Results may differ from a plain program's by a relative error of at most 0.00013.
Values sent between devices are 32-bit elements; how exact they have to be, the bound alone decides.
No kernel may reach another device: no remote copies, remote signals or barrier semaphores. Data moves between devices by JAX's collectives and lax.ppermute only.
A program may use at most 128 MiB of HBM per device.

v0:
```python
import jax
import jax.numpy as jnp
from jax import lax
from jax.sharding import PartitionSpec as P

B = 4096
STEPS = 2
ridge_weight = 0.5
kernel_scale = 0.125


def from_root(value, axis, source):
    kept = jnp.where(lax.axis_index(axis) == source, value, 0).astype(value.dtype)
    return lax.psum(kept, axis)


def body(points, residual, coef, block_of, order, inverse):
    highest = lax.Precision.HIGHEST
    n_mem = lax.axis_size("mem")
    per = B // (lax.axis_size("grp") * n_mem)
    slots = inverse.shape[0]
    mine = lax.axis_index("grp") * n_mem + lax.axis_index("mem")
    norms_local = jnp.sum(points * points, axis=0)
    for step_index in range(STEPS):
        block_id = order[step_index]
        inside = block_of == block_id
        position = jnp.cumsum(inside.astype(jnp.int32)) - 1
        select = (
            (position[:, None] == jnp.arange(per, dtype=jnp.int32)[None, :]) & inside[:, None]
        ).astype(jnp.float32)
        chosen_res = jnp.dot(residual, select, precision=highest)
        chosen_pts = jnp.dot(points, select, precision=highest)
        block_res, block_pts = (
            lax.all_gather(chosen_res, ("grp", "mem"), axis=1, tiled=True),
            lax.all_gather(chosen_pts, ("grp", "mem"), axis=1, tiled=True),
        )
        matrix_rows = lax.dynamic_index_in_dim(inverse, block_id % slots, 0, keepdims=False)
        solved = lax.dot_general(
            block_res, matrix_rows, (((1,), (1,)), ((), ())), precision=highest
        )
        owner = block_id // slots
        norms_block = jnp.sum(block_pts * block_pts, axis=0)
        assembled = lax.all_gather(solved, "mem", axis=1, tiled=True)
        assembled = from_root(assembled, "grp", owner)
        width = assembled.shape[1]
        cross = lax.dot_general(points, block_pts, (((0,), (0,)), ((), ())), precision=highest)
        kernel = jnp.exp(
            -kernel_scale * (norms_local[:, None] + norms_block[None, :] - 2.0 * cross)
        )
        total_update = lax.dot_general(
            assembled, kernel, (((1,), (1,)), ((), ())), precision=highest
        )
        ranks = jnp.arange(width, dtype=jnp.int32)
        wanted = mine * per + jnp.arange(per, dtype=jnp.int32)
        picker = (ranks[:, None] == wanted[None, :]).astype(jnp.float32)
        owned = jnp.dot(assembled, picker, precision=highest)
        update, owned = (total_update, owned)
        spread_back = lax.dot_general(owned, select, (((1,), (1,)), ((), ())), precision=highest)
        residual = residual - update - ridge_weight * spread_back
        coef = coef + spread_back
    return (residual, coef)


def solution(mesh):
    in_specs = (
        P(None, ("grp", "mem")),
        P(None, ("grp", "mem")),
        P(None, ("grp", "mem")),
        P(("grp", "mem")),
        P(),
        P("grp", "mem", None),
    )
    out_specs = (P(None, ("grp", "mem")), P(None, ("grp", "mem")))
    return jax.shard_map(body, mesh=mesh, in_specs=in_specs, out_specs=out_specs, check_vma=False)
```

profile of v0, /device:TPU:0, one launch (start us, length us, event | category | flops | bytes accessed | tf_op | source)
XLA Modules:
  0.0 461.2 jit_solution(17110810315561444372)
XLA Ops:
  7.2 1.3 fusion.67
  8.5 2.0 convert_bitcast_fusion
  11.1 1.4 convolution_bitcast_fusion.2
  12.5 71.8 %all_gather.18 = f32[16,4096]{1,0:T(8,128)S(1)} all-gather(f32[16,128]{1,0:T(8,128)S(1)} %convolution_bitcast_fusion.2), channel_id=1, replica_groups=mesh['grp'=8,'mem'=4] {'grp','mem'}, dimensions={1}, use_global_device_ids=true | all-gather | bytes 270336 | tf_op jit(solution)/shard_map/all_gather | solution.py:34
  84.3 17.1 %fusion.10 = f32[16,1024]{1,0:T(8,128)S(1)} fusion(f32[16,4096]{1,0:T(8,128)S(1)} %all_gather.18, f32[1,1024,4096]{2,1,0:T(8,128)} %param.11), kind=kOutput, calls=%fused_computation.10 | convolution fusion | flops 805306368 | bytes 17104896 | tf_op jit(solution)/shard_map/dot_general | solution.py:38
  101.4 14.3 %all_gather.19 = f32[16,4096]{1,0:T(8,128)S(1)} all-gather(f32[16,1024]{1,0:T(8,128)S(1)} %fusion.10), channel_id=1, replica_groups=mesh['grp'=8,'mem'=4] {'mem'}, dimensions={1}, use_global_device_ids=true | all-gather | bytes 327680 | tf_op jit(solution)/shard_map/all_gather | solution.py:43
  116.4 0.7 broadcast_select_fusion.1
  117.2 0.5 convolution_bitcast_fusion.1
  117.7 65.6 %all_gather.20 = f32[16,4096]{1,0:T(8,128)S(1)} all-gather(f32[16,128]{1,0:T(8,128)S(1)} %convolution_bitcast_fusion.1), channel_id=1, replica_groups=mesh['grp'=8,'mem'=4] {'grp','mem'}, dimensions={1}, use_global_device_ids=true | all-gather | bytes 270336 | tf_op jit(solution)/shard_map/all_gather | solution.py:35
  183.3 15.9 %fusion.68 = f32[4096,1024]{1,0:T(8,128)} fusion(f32[16,4096]{1,0:T(8,128)S(1)} %all_gather.20, f32[16,1024]{1,0:T(8,128)S(1)} %copy-done), kind=kOutput, calls=%fused_computation.75 | convolution fusion | flops 805306368 | bytes 17104896 | tf_op jit(solution)/shard_map/dot_general | solution.py:46
  199.8 0.5 convolution_bitcast_fusion
  201.0 67.7 %all_gather.23 = f32[16,4096]{1,0:T(8,128)S(1)} all-gather(f32[16,128]{1,0:T(8,128)S(1)} %convolution_bitcast_fusion), channel_id=1, replica_groups=mesh['grp'=8,'mem'=4] {'grp','mem'}, dimensions={1}, use_global_device_ids=true | all-gather | bytes 270336 | tf_op jit(solution)/shard_map/all_gather | solution.py:35
  268.7 1.7 fusion.25
  270.5 1.2 fusion.41
  271.6 14.8 %fusion.29 = f32[16,1024]{1,0:T(8,128)S(1)} fusion(f32[16,1024]{1,0:T(8,128)S(1)} %copy-done.1, f32[16,4096]{1,0:T(8,128)} %all-reduce.3.cloned.1.call-done, f32[4096,1024]{1,0:T(8,128)} %fusion.68, f32[4096]{0:T(1024)S(1)} %multiply_reduce_fusion.1, f32[1024]{0:T(1024)S(1)} %multiply_reduce_fusion.2, f32[16,1024]{1,0:T(8,128)S(1)} %fusion.41), kind=kOutput, calls=%fused_computation.28 | convolution fusion | flops 822132736 | bytes 17256448 | tf_op jit(solution)/shard_map/dot_general | solution.py:50
  286.9 65.5 %all_gather.21 = f32[16,4096]{1,0:T(8,128)S(1)} all-gather(f32[16,128]{1,0:T(8,128)S(1)} %fusion.49), channel_id=1, replica_groups=mesh['grp'=8,'mem'=4] {'grp','mem'}, dimensions={1}, use_global_device_ids=true | all-gather | bytes 270336 | tf_op jit(solution)/shard_map/all_gather | solution.py:34
  352.4 17.2 %fusion.8 = f32[16,1024]{1,0:T(8,128)S(1)} fusion(f32[16,4096]{1,0:T(8,128)S(1)} %all_gather.21, f32[1,1024,4096]{2,1,0:T(8,128)} %param.11), kind=kOutput, calls=%fused_computation.8 | convolution fusion | flops 805306368 | bytes 17104896 | tf_op jit(solution)/shard_map/dot_general | solution.py:38
  369.6 14.3 %all_gather.22 = f32[16,4096]{1,0:T(8,128)S(1)} all-gather(f32[16,1024]{1,0:T(8,128)S(1)} %fusion.8), channel_id=1, replica_groups=mesh['grp'=8,'mem'=4] {'mem'}, dimensions={1}, use_global_device_ids=true | all-gather | bytes 327680 | tf_op jit(solution)/shard_map/all_gather | solution.py:43
  383.9 0.7 broadcast_select_fusion
  384.6 15.9 %fusion.69 = f32[4096,1024]{1,0:T(8,128)} fusion(f32[16,4096]{1,0:T(8,128)S(1)} %all_gather.23, f32[16,1024]{1,0:T(8,128)S(1)} %copy-done), kind=kOutput, calls=%fused_computation.76 | convolution fusion | flops 805306368 | bytes 17104896 | tf_op jit(solution)/shard_map/dot_general | solution.py:46
  400.6 35.4 %all-reduce.5.cloned.1.call-done = f32[16,4096]{1,0:T(8,128)} async-done(((f32[16,4096]{1,0:T(8,128)}), f32[16,4096]{1,0:T(8,128)}) %all-reduce.5.cloned.1.call-update) | async-done | bytes 262160 | tf_op jit(solution)/shard_map/psum | solution.py:14
  436.0 1.7 fusion.24
  437.8 1.2 add_add_fusion
  439.0 15.4 %fusion.35 = f32[16,1024]{1,0:T(8,128)} fusion(f32[16,1024]{1,0:T(8,128)S(1)} %fusion.29, f32[16,4096]{1,0:T(8,128)} %all-reduce.5.cloned.1.call-done, f32[4096,1024]{1,0:T(8,128)} %fusion.69, f32[4096]{0:T(1024)S(1)} %multiply_reduce_fusion, f32[1024]{0:T(1024)S(1)} %multiply_reduce_fusion.2, f32[16,1024]{1,0:T(8,128)S(1)} %get-tuple-element.11), kind=kOutput, calls=%fused_computation.30 | convolution fusion | flops 822132736 | bytes 17256448 | tf_op jit(solution)/shard_map/dot_general | solution.py:50
  (26 shorter events, 1.9 us)
Async XLA Ops:
  7.2 110.0 %copy-start = (f32[16,1024]{1,0:T(8,128)S(1)}, f32[16,1024]{1,0:T(8,128)}, u32[]{:S(2)}) copy-start(f32[16,1024]{1,0:T(8,128)} %param.6) | copy-start | bytes 196612
  7.2 261.5 %all-reduce.3.cloned.1.call-start = ((), (), s32[]{:S(2)}) async-start(), calls=%async_computation | async-start | bytes 524288 | tf_op jit(solution)/shard_map/psum | solution.py:14
  101.4 170.2 %copy-start.1 = (f32[16,1024]{1,0:T(8,128)S(1)}, f32[16,1024]{1,0:T(8,128)}, u32[]{:S(2)}) copy-start(f32[16,1024]{1,0:T(8,128)} %param.7) | copy-start | bytes 196612
  117.1 318.9 %all-reduce.5.cloned.1.call-start = ((), (), s32[]{:S(2)}) async-start(), calls=%async_computation.1 | async-start | bytes 524288 | tf_op jit(solution)/shard_map/psum | solution.py:14
  352.4 85.3 %copy-start.2 = (f32[16,1024]{1,0:T(8,128)S(1)}, f32[16,1024]{1,0:T(8,128)}, u32[]{:S(2)}) copy-start(f32[16,1024]{1,0:T(8,128)} %param.8) | copy-start | bytes 196612
Sparse Core Ops, SparseCore 0:
  117.3 49.9 all-reduce.2
  384.7 51.2 all-reduce.4
where the time goes:
time: 462 us; the launch traced here: 461 us
  blocking collectives  299 us (65%)
  matrix products  105 us (23%)
  waiting for transfers between devices  35.5 us (8%)
  between operations  15.5 us (3%)
    all_gather x2, blocking collectives, body(): lax.all_gather(chosen_res, ('grp', 'mem'), axis=1, tiled=True)  137 us
    all_gather x2, blocking collectives, body(): lax.all_gather(chosen_pts, ('grp', 'mem'), axis=1, tiled=True)  133 us
    psum x2, waiting for transfers between devices, from_root(): return lax.psum(kept, axis)  35.4 us
    dot_general x2, matrix products, body(): lax.dot_general(block_res, matrix_rows, (((1,), (1,)), ((), ())), precisi...  34.3 us
    dot_general x2, matrix products, body(): lax.dot_general(points, block_pts, (((0,), (0,)), ((), ())), precision=hi...  31.8 us
    dot_general x2, matrix products, body(): lax.dot_general(assembled, kernel, (((1,), (1,)), ((), ())), precision=hi...  30.2 us
    all_gather x2, blocking collectives, body(): assembled = lax.all_gather(solved, 'mem', axis=1, tiled=True)  28.6 us
  transfers between devices with their start and end apart: 2, of which 1 were waited for; matrix products, arithmetic and copies ran while one was open for 7% of the time, Pallas kernels for 0%

commit v1 on v0

--- a/solution.py
+++ b/solution.py
@@ -11,7 +11,7 @@
 
 def from_root(value, axis, source):
     kept = jnp.where(lax.axis_index(axis) == source, value, 0).astype(value.dtype)
-    return lax.psum(kept, axis)
+    return jnp.sum(lax.all_gather(kept, axis), axis=0)
 
 
 def body(points, residual, coef, block_of, order, inverse):

time: 462 us -> 427 us (0.924)
  waiting for transfers between devices: 35.5 us -> 0.04 us
    psum x2 -> x0, waiting for transfers between devices: 35.4 us -> none  [from_root(): return lax.psum(kept, axis)]
  transfers between devices with their start and end apart: 2 -> 2, of which waited for: 1 -> 0; matrix products, arithmetic and copies ran while one was open for 7% -> 8% of each run, Pallas kernels for 0% -> 0%
where the time goes in v1:
time: 427 us; the launch traced here: 426 us
  blocking collectives  300 us (70%)
  matrix products  101 us (24%)
  between operations  15.5 us (4%)
  other arithmetic  7.76 us (2%)
    all_gather x2, blocking collectives, body(): lax.all_gather(chosen_res, ('grp', 'mem'), axis=1, tiled=True)  140 us
    all_gather x2, blocking collectives, body(): lax.all_gather(chosen_pts, ('grp', 'mem'), axis=1, tiled=True)  132 us
    dot_general x2, matrix products, body(): lax.dot_general(block_res, matrix_rows, (((1,), (1,)), ((), ())), precisi...  34.3 us
    dot_general x2, matrix products, body(): lax.dot_general(points, block_pts, (((0,), (0,)), ((), ())), precision=hi...  31.8 us
    dot_general x2, matrix products, body(): lax.dot_general(assembled, kernel, (((1,), (1,)), ((), ())), precision=hi...  28.4 us
    all_gather x2, blocking collectives, body(): assembled = lax.all_gather(solved, 'mem', axis=1, tiled=True)  28.4 us
  transfers between devices with their start and end apart: 2, of which 0 were waited for; matrix products, arithmetic and copies ran while one was open for 8% of the time, Pallas kernels for 0%

profile of v1, /device:TPU:0, one launch (start us, length us, event | category | flops | bytes accessed | tf_op | source)
XLA Modules:
  0.0 426.2 jit_solution(1991397366311001406)
XLA Ops:
  7.2 1.3 fusion.67
  8.5 2.0 convert_bitcast_fusion
  11.1 1.4 convolution_bitcast_fusion.2
  12.5 71.8 %all_gather.30 = f32[16,4096]{1,0:T(8,128)S(1)} all-gather(f32[16,128]{1,0:T(8,128)S(1)} %convolution_bitcast_fusion.2), channel_id=1, replica_groups=mesh['grp'=8,'mem'=4] {'grp','mem'}, dimensions={1}, use_global_device_ids=true | all-gather | bytes 270336 | tf_op jit(solution)/shard_map/all_gather | solution.py:34
  84.3 17.1 %fusion.10 = f32[16,1024]{1,0:T(8,128)S(1)} fusion(f32[16,4096]{1,0:T(8,128)S(1)} %all_gather.30, f32[1,1024,4096]{2,1,0:T(8,128)} %param.11), kind=kOutput, calls=%fused_computation.10 | convolution fusion | flops 805306368 | bytes 17104896 | tf_op jit(solution)/shard_map/dot_general | solution.py:38
  101.4 14.2 %all_gather.31 = f32[16,4096]{1,0:T(8,128)S(1)} all-gather(f32[16,1024]{1,0:T(8,128)S(1)} %fusion.10), channel_id=1, replica_groups=mesh['grp'=8,'mem'=4] {'mem'}, dimensions={1}, use_global_device_ids=true | all-gather | bytes 327680 | tf_op jit(solution)/shard_map/all_gather | solution.py:43
  116.2 0.7 broadcast_select_fusion.1
  118.2 0.5 convolution_bitcast_fusion.1
  118.8 65.9 %all_gather.34 = f32[16,4096]{1,0:T(8,128)S(1)} all-gather(f32[16,128]{1,0:T(8,128)S(1)} %convolution_bitcast_fusion.1), channel_id=1, replica_groups=mesh['grp'=8,'mem'=4] {'grp','mem'}, dimensions={1}, use_global_device_ids=true | all-gather | bytes 270336 | tf_op jit(solution)/shard_map/all_gather | solution.py:35
  184.8 15.9 %fusion.68 = f32[4096,1024]{1,0:T(8,128)} fusion(f32[16,4096]{1,0:T(8,128)S(1)} %all_gather.34, f32[16,1024]{1,0:T(8,128)S(1)} %copy-done), kind=kOutput, calls=%fused_computation.75 | convolution fusion | flops 805306368 | bytes 17104896 | tf_op jit(solution)/shard_map/dot_general | solution.py:46
  200.7 1.7 reduce_sum.45
  202.4 0.8 fusion.25
  203.2 1.2 fusion.41
  204.4 13.9 %fusion.29 = f32[16,1024]{1,0:T(8,128)S(1)} fusion(f32[16,1024]{1,0:T(8,128)S(1)} %copy-done.1, f32[16,4096]{1,0:T(8,128)S(1)} %reduce_sum.45, f32[4096,1024]{1,0:T(8,128)} %fusion.68, f32[4096]{0:T(1024)S(1)} %multiply_reduce_fusion.1, f32[1024]{0:T(1024)S(1)} %multiply_reduce_fusion.2, f32[16,1024]{1,0:T(8,128)S(1)} %fusion.41), kind=kOutput, calls=%fused_computation.28 | convolution fusion | flops 822132736 | bytes 17256448 | tf_op jit(solution)/shard_map/dot_general | solution.py:50
  218.8 67.8 %all_gather.35 = f32[16,4096]{1,0:T(8,128)S(1)} all-gather(f32[16,128]{1,0:T(8,128)S(1)} %fusion.49), channel_id=1, replica_groups=mesh['grp'=8,'mem'=4] {'grp','mem'}, dimensions={1}, use_global_device_ids=true | all-gather | bytes 270336 | tf_op jit(solution)/shard_map/all_gather | solution.py:34
  286.6 17.1 %fusion.8 = f32[16,1024]{1,0:T(8,128)S(1)} fusion(f32[16,4096]{1,0:T(8,128)S(1)} %all_gather.35, f32[1,1024,4096]{2,1,0:T(8,128)} %param.11), kind=kOutput, calls=%fused_computation.8 | convolution fusion | flops 805306368 | bytes 17104896 | tf_op jit(solution)/shard_map/dot_general | solution.py:38
  303.7 14.2 %all_gather.36 = f32[16,4096]{1,0:T(8,128)S(1)} all-gather(f32[16,1024]{1,0:T(8,128)S(1)} %fusion.8), channel_id=1, replica_groups=mesh['grp'=8,'mem'=4] {'mem'}, dimensions={1}, use_global_device_ids=true | all-gather | bytes 327680 | tf_op jit(solution)/shard_map/all_gather | solution.py:43
  317.9 0.7 broadcast_select_fusion
  319.2 66.0 %all_gather.39 = f32[16,4096]{1,0:T(8,128)S(1)} all-gather(f32[16,128]{1,0:T(8,128)S(1)} %convolution_bitcast_fusion), channel_id=1, replica_groups=mesh['grp'=8,'mem'=4] {'grp','mem'}, dimensions={1}, use_global_device_ids=true | all-gather | bytes 270336 | tf_op jit(solution)/shard_map/all_gather | solution.py:35
  385.2 15.9 %fusion.69 = f32[4096,1024]{1,0:T(8,128)} fusion(f32[16,4096]{1,0:T(8,128)S(1)} %all_gather.39, f32[16,1024]{1,0:T(8,128)S(1)} %copy-done), kind=kOutput, calls=%fused_computation.76 | convolution fusion | flops 805306368 | bytes 17104896 | tf_op jit(solution)/shard_map/dot_general | solution.py:46
  401.1 1.7 reduce_sum.48
  402.8 0.8 fusion.24
  403.6 1.2 add_add_fusion
  404.9 14.5 %fusion.35 = f32[16,1024]{1,0:T(8,128)} fusion(f32[16,1024]{1,0:T(8,128)S(1)} %fusion.29, f32[16,4096]{1,0:T(8,128)S(1)} %reduce_sum.48, f32[4096,1024]{1,0:T(8,128)} %fusion.69, f32[4096]{0:T(1024)S(1)} %multiply_reduce_fusion, f32[1024]{0:T(1024)S(1)} %multiply_reduce_fusion.2, f32[16,1024]{1,0:T(8,128)S(1)} %get-tuple-element.11), kind=kOutput, calls=%fused_computation.30 | convolution fusion | flops 822132736 | bytes 17256448 | tf_op jit(solution)/shard_map/dot_general | solution.py:50
  (28 shorter events, 2.4 us)
Async XLA Ops:
  7.2 111.0 %copy-start = (f32[16,1024]{1,0:T(8,128)S(1)}, f32[16,1024]{1,0:T(8,128)}, u32[]{:S(2)}) copy-start(f32[16,1024]{1,0:T(8,128)} %param.6) | copy-start | bytes 196612
  7.2 193.5 %all-gather.5.cloned.1.call-start = ((), (), s32[]{:S(2)}) async-start(), calls=%async_computation | async-start | bytes 2359296 | tf_op jit(solution)/shard_map/all_gather | solution.py:14
  101.4 103.0 %copy-start.1 = (f32[16,1024]{1,0:T(8,128)S(1)}, f32[16,1024]{1,0:T(8,128)}, u32[]{:S(2)}) copy-start(f32[16,1024]{1,0:T(8,128)} %param.7) | copy-start | bytes 196612
  117.0 284.1 %all-gather.7.cloned.1.call-start = ((), (), s32[]{:S(2)}) async-start(), calls=%async_computation.1 | async-start | bytes 2359296 | tf_op jit(solution)/shard_map/all_gather | solution.py:14
  303.7 99.9 %copy-start.2 = (f32[16,1024]{1,0:T(8,128)S(1)}, f32[16,1024]{1,0:T(8,128)}, u32[]{:S(2)}) copy-start(f32[16,1024]{1,0:T(8,128)} %param.8) | copy-start | bytes 196612
Sparse Core Ops, SparseCore 0:
  117.1 24.4 all-gather.4
  318.8 24.3 all-gather.6
